TPU v7x, 512 devices: a whole 4x4x16 slice. The times are simulated.
512 devices in a mesh: row: 16 (over z), col: 32 (over y, x, core).
Axes of the slice: x: 4, y: 4, z: 16, core: 2. Of those that a mesh axis runs over, the one named last changes fastest.
Arguments:
- inputs: bfloat16 [2048, 8192], P('col', 'row'), may hold values from -6 to 6
- gate_pre: bfloat16 [2048, 14784], P('row', 'col'), may hold values from -6 to 6
- up_pre: bfloat16 [2048, 14784], P('row', 'col'), may hold values from -6 to 6
- w_gate: bfloat16 [8192, 14784], P('row', 'col'), may hold values from -0.0625 to 0.0625
- w_up: bfloat16 [8192, 14784], P('row', 'col'), may hold values from -0.0625 to 0.0625
- w_down: bfloat16 [14784, 8192], P('col', 'row'), may hold values from -0.046875 to 0.046875
- grad_out: bfloat16 [2048, 8192], P('col', 'row'), may hold values from -1.5 to 1.5
Outputs:
- grad_in: bfloat16 [2048, 8192], P('col', 'row')
- grad_gate: bfloat16 [8192, 14784], P('row', 'col')
- grad_up: bfloat16 [8192, 14784], P('row', 'col')
- grad_down: bfloat16 [14784, 8192], P('col', 'row')
All inputs are finite; a program needn't handle non-finite values.
Results may differ from a plain program's by a relative error of at most 0.025.
Values may be sent and summed in bfloat16 or wider, within the bound.
No kernel may reach another device: no remote copies, remote signals or barrier semaphores. Data moves between devices by JAX's collectives and lax.ppermute only.
A program may use at most 64 MiB of HBM per device.

v0:
```python
import jax
import jax.numpy as jnp
from jax import lax
from jax.sharding import PartitionSpec as P


def contract_rows(left, right):
    return lax.dot_general(
        left, right, (((0,), (0,)), ((), ())), preferred_element_type=jnp.float32
    )


def contract_cols(left, right):
    return lax.dot_general(
        left, right, (((1,), (1,)), ((), ())), preferred_element_type=jnp.float32
    )


def pointwise(gate_pre, up_pre, hidden_grad):
    gate_value = gate_pre.astype(jnp.float32)
    up_value = up_pre.astype(jnp.float32)
    sigmoid_gate = jax.nn.sigmoid(gate_value)
    activated = gate_value * sigmoid_gate
    hidden = (activated * up_value).astype(jnp.bfloat16)
    up_grad = (hidden_grad * activated).astype(jnp.bfloat16)
    gate_grad = (
        hidden_grad * up_value * sigmoid_gate * (1.0 + gate_value * (1.0 - sigmoid_gate))
    ).astype(jnp.bfloat16)
    return (hidden, gate_grad, up_grad)


def shards(inputs, gate_pre, up_pre, w_gate, w_up, w_down, grad_out):
    all_grad_out, all_inputs = (
        lax.all_gather(grad_out, "col", axis=0, tiled=True),
        lax.all_gather(inputs, "col", axis=0, tiled=True),
    )
    hidden_grad = lax.psum_scatter(
        contract_cols(all_grad_out, w_down).astype(jnp.bfloat16),
        "row",
        scatter_dimension=0,
        tiled=True,
    ).astype(jnp.float32)
    share_hidden, share_gate, share_up = pointwise(gate_pre, up_pre, hidden_grad)
    hidden, gate_grad, up_grad = (
        lax.all_gather(share_hidden, "row", axis=0, tiled=True),
        lax.all_gather(share_gate, "row", axis=0, tiled=True),
        lax.all_gather(share_up, "row", axis=0, tiled=True),
    )
    grad_down = contract_rows(hidden, all_grad_out).astype(jnp.bfloat16)
    grad_gate = contract_rows(all_inputs, gate_grad).astype(jnp.bfloat16)
    grad_up = contract_rows(all_inputs, up_grad).astype(jnp.bfloat16)
    grad_in = lax.psum_scatter(
        (contract_cols(gate_grad, w_gate) + contract_cols(up_grad, w_up)).astype(jnp.bfloat16),
        "col",
        scatter_dimension=0,
        tiled=True,
    )
    return (grad_in, grad_gate, grad_up, grad_down)


def solution(mesh):
    return jax.shard_map(
        shards,
        mesh=mesh,
        in_specs=(
            P("col", "row"),
            P("row", "col"),
            P("row", "col"),
            P("row", "col"),
            P("row", "col"),
            P("col", "row"),
            P("col", "row"),
        ),
        out_specs=(P("col", "row"), P("row", "col"), P("row", "col"), P("col", "row")),
        check_vma=False,
    )
```

profile of v0, /device:TPU:2, one launch (start us, length us, event | category | flops | bytes accessed | tf_op | source)
XLA Modules:
  0.0 553.4 jit_solution(13441405227481804049)
XLA Ops:
  7.2 0.0 copy-start
  7.2 0.0 all-gather.6.cloned.1.call-start
  7.2 0.7 all-gather.6.cloned.1.call-update
  7.9 0.0 reduce-scatter.7.cloned.1.call-start
  8.0 66.2 %all-gather.6.cloned.1.call-done = bf16[2048,512]{1,0:T(8,128)(2,1)} async-done(((bf16[64,512]{1,0:T(8,128)(2,1)}), bf16[2048,512]{1,0:T(8,128)(2,1)}) %all-gather.6.cloned.1.call-update) | async-done | bytes 2097168 | tf_op jit(solution)/shard_map/all_gather | solution.py:34
  74.2 2.8 convolution_convert_fusion
  77.0 2.5 copy.11
  79.5 0.0 copy-start.3
  79.5 0.0 copy-start.4
  79.5 0.0 reduce-scatter.7.cloned.1.call-update
  79.5 0.0 all-gather.8.cloned.1.call-start
  79.6 73.9 %reduce-scatter.7.cloned.1.call-done = bf16[128,462]{1,0:T(8,128)(2,1)} async-done(((bf16[2048,462]{1,0:T(8,128)(2,1)}), bf16[128,462]{1,0:T(8,128)(2,1)}) %reduce-scatter.7.cloned.1.call-update) | async-done | bytes 118288
  153.5 1.0 copy.12
  154.5 0.0 copy-done.3
  154.5 0.0 copy-done.4
  154.5 0.9 fusion.6
  155.4 0.0 all-gather.8.cloned.1.call-update
  155.4 0.0 all-gather.10.cloned.1.call-start
  155.5 0.5 all-gather.10.cloned.1.call-update
  156.0 0.0 all-gather.12.cloned.1.call-start
  156.0 0.5 all-gather.12.cloned.1.call-update
  156.6 0.0 all-gather.14.cloned.1.call-start
  156.6 0.5 all-gather.14.cloned.1.call-update
  157.1 0.0 copy-start.2
  157.2 0.0 reduce-scatter.5.cloned.1.call-start
  157.2 73.9 %all-gather.8.cloned.1.call-done = bf16[2048,462]{0,1:T(8,128)(2,1)} async-done(((bf16[128,462]{0,1:T(8,128)(2,1)}), bf16[2048,462]{0,1:T(8,128)(2,1)}) %all-gather.8.cloned.1.call-update) | async-done | bytes 1892368 | tf_op jit(solution)/shard_map/all_gather | solution.py:46
  231.1 0.0 copy-done
  231.1 4.8 fusion.11
  235.8 71.0 %all-gather.10.cloned.1.call-done = bf16[2048,462]{0,1:T(8,128)(2,1)} async-done(((bf16[128,462]{0,1:T(8,128)(2,1)}), bf16[2048,462]{0,1:T(8,128)(2,1)}) %all-gather.10.cloned.1.call-update) | async-done | bytes 1892368 | tf_op jit(solution)/shard_map/all_gather | solution.py:47
  306.8 0.0 copy-done.2
  306.8 5.5 add_convert_fusion
  312.3 0.0 reduce-scatter.5.cloned.1.call-update
  312.3 0.0 copy-start.1
  312.3 51.9 %all-gather.12.cloned.1.call-done = bf16[2048,512]{1,0:T(8,128)(2,1)} async-done(((bf16[64,512]{1,0:T(8,128)(2,1)}), bf16[2048,512]{1,0:T(8,128)(2,1)}) %all-gather.12.cloned.1.call-update) | async-done | bytes 2097168 | tf_op jit(solution)/shard_map/all_gather | solution.py:35
  364.3 0.0 copy-start.5
  364.3 4.2 fusion.1
  368.5 0.0 copy-done.1
  368.5 0.0 copy-done.5
  368.5 1.9 fusion
  370.4 73.5 %all-gather.14.cloned.1.call-done = bf16[2048,462]{0,1:T(8,128)(2,1)} async-done(((bf16[128,462]{0,1:T(8,128)(2,1)}), bf16[2048,462]{0,1:T(8,128)(2,1)}) %all-gather.14.cloned.1.call-update) | async-done | bytes 1892368 | tf_op jit(solution)/shard_map/all_gather | solution.py:45
  444.0 4.1 convolution_convert_fusion.1
  448.0 98.5 %reduce-scatter.5.cloned.1.call-done = bf16[64,512]{1,0:T(8,128)(2,1)} async-done(((bf16[2048,512]{1,0:T(8,128)(2,1)}), bf16[64,512]{1,0:T(8,128)(2,1)}) %reduce-scatter.5.cloned.1.call-update) | async-done | bytes 65552 | tf_op jit(solution)/shard_map/reduce_scatter | solution.py:52
Async XLA Ops:
  7.2 223.9 %copy-start = (bf16[512,462]{0,1:T(8,128)(2,1)S(1)}, bf16[512,462]{0,1:T(8,128)(2,1)}, u32[]{:S(2)}) copy-start(bf16[512,462]{0,1:T(8,128)(2,1)} %param.10) | copy-start | bytes 1419268
  7.2 67.0 %all-gather.6.cloned.1.call-start = ((), (), s32[]{:S(2)}) async-start(), calls=%async_computation.2 | async-start | bytes 2162688 | tf_op jit(solution)/shard_map/all_gather | solution.py:34
  7.9 145.5 %reduce-scatter.7.cloned.1.call-start = ((), (), s32[]{:S(2)}) async-start(), calls=%async_computation.8 | async-start | bytes 2228224
  79.5 75.0 %copy-start.3 = (bf16[128,462]{0,1:T(8,128)(2,1)S(1)}, bf16[128,462]{0,1:T(8,128)(2,1)}, u32[]{:S(2)}) copy-start(bf16[128,462]{0,1:T(8,128)(2,1)} %param.9) | copy-start | bytes 354820
  79.5 75.0 %copy-start.4 = (bf16[128,462]{0,1:T(8,128)(2,1)S(1)}, bf16[128,462]{0,1:T(8,128)(2,1)}, u32[]{:S(2)}) copy-start(bf16[128,462]{0,1:T(8,128)(2,1)} %param.8) | copy-start | bytes 354820
  79.5 151.6 %all-gather.8.cloned.1.call-start = ((), (), s32[]{:S(2)}) async-start(), calls=%async_computation.3 | async-start | bytes 2019328 | tf_op jit(solution)/shard_map/all_gather | solution.py:46
  155.4 151.4 %all-gather.10.cloned.1.call-start = ((), (), s32[]{:S(2)}) async-start(), calls=%async_computation.4 | async-start | bytes 2019328 | tf_op jit(solution)/shard_map/all_gather | solution.py:47
  156.0 208.3 %all-gather.12.cloned.1.call-start = ((), (), s32[]{:S(2)}) async-start(), calls=%async_computation.6 | async-start | bytes 2162688 | tf_op jit(solution)/shard_map/all_gather | solution.py:35
  156.6 287.4 %all-gather.14.cloned.1.call-start = ((), (), s32[]{:S(2)}) async-start(), calls=%async_computation.7 | async-start | bytes 2019328 | tf_op jit(solution)/shard_map/all_gather | solution.py:45
  157.1 149.7 %copy-start.2 = (bf16[512,462]{0,1:T(8,128)(2,1)S(1)}, bf16[512,462]{0,1:T(8,128)(2,1)}, u32[]{:S(2)}) copy-start(bf16[512,462]{0,1:T(8,128)(2,1)} %param.11) | copy-start | bytes 1419268
  157.2 389.4 %reduce-scatter.5.cloned.1.call-start = ((), (), s32[]{:S(2)}) async-start(), calls=%async_computation.5 | async-start | bytes 2162688 | tf_op jit(solution)/shard_map/reduce_scatter | solution.py:52
  312.3 56.2 %copy-start.1 = (bf16[2048,462]{0,1:T(8,128)(2,1)S(1)}, bf16[2048,462]{0,1:T(8,128)(2,1)}, u32[]{:S(2)}) copy-start(bf16[2048,462]{0,1:T(8,128)(2,1)} %all-gather.8.cloned.1.call-done) | copy-start | bytes 5677060
  364.3 4.2 copy-start.5
Sparse Core Ops, SparseCore 0:
  11.1 63.0 all-gather.5
  79.6 73.7 reduce-scatter.6
  156.0 74.9 all-gather.7
  233.5 73.2 all-gather.9
  309.8 54.3 all-gather.11
  366.7 77.2 all-gather.13
  448.9 97.5 reduce-scatter.4
where the time goes:
time: 554 us; the launch traced here: 553 us
  waiting for transfers between devices  511 us (92%)
  matrix products  23.3 us (4%)
  between operations  14.2 us (3%)
    reduce_scatter x1, waiting for transfers between devices, shards(): lax.psum_scatter((contract_cols(gate_grad, w_gate) + contract_cols(up_gra...  98.5 us
    unnamed x8, waiting for transfers between devices  76.2 us
    all_gather x1, waiting for transfers between devices, shards(): lax.all_gather(share_gate, 'row', axis=0, tiled=True)  73.9 us
    all_gather x1, waiting for transfers between devices, shards(): lax.all_gather(share_hidden, 'row', axis=0, tiled=True)  73.5 us
    all_gather x1, waiting for transfers between devices, shards(): lax.all_gather(share_up, 'row', axis=0, tiled=True)  71 us
    all_gather x1, waiting for transfers between devices, shards(): lax.all_gather(grad_out, 'col', axis=0, tiled=True)  66.2 us
    all_gather x1, waiting for transfers between devices, shards(): lax.all_gather(inputs, 'col', axis=0, tiled=True)  51.9 us
    dot_general x3, matrix products, contract_cols(): lax.dot_general(left, right, (((1,), (1,)), ((), ())), preferred_element_...  13.1 us
  transfers between devices with their start and end apart: 7, of which 7 were waited for; matrix products, arithmetic and copies ran while one was open for 4% of the time, Pallas kernels for 0%

commit v1 on v0

--- a/solution.py
+++ b/solution.py
@@ -30,8 +30,15 @@
 
 
 def shards(inputs, gate_pre, up_pre, w_gate, w_up, w_down, grad_out):
+
+    def _clear_skins(point, d_out):
+        row_out = jnp.concatenate(
+            lax.all_to_all(jnp.stack([point] * lax.psum(1, "col")), "col", 0, 0), d_out
+        )
+        return row_out
+
     all_grad_out, all_inputs = (
-        lax.all_gather(grad_out, "col", axis=0, tiled=True),
+        _clear_skins(grad_out, 0),
         lax.all_gather(inputs, "col", axis=0, tiled=True),
     )
     hidden_grad = lax.psum_scatter(

time: 554 us -> 524 us (0.946)
  waiting for transfers between devices: 511 us -> 445 us
  blocking collectives: 0 us -> 36 us
    all_gather x1 -> x0, waiting for transfers between devices: 66.2 us -> none  [shards(): lax.all_gather(grad_out, 'col', axis=0, tiled=True)]
    all_to_all x0 -> x1, blocking collectives: none -> 36 us  [_clear_skins(): lax.all_to_all(jnp.stack([point] * lax.psum(1, 'col')), 'col', 0, 0)]
    unnamed x8 -> x7, waiting for transfers between devices: 76.2 us -> 76.4 us
  transfers between devices with their start and end apart: 7 -> 6, of which waited for: 7 -> 6; matrix products, arithmetic and copies ran while one was open for 4% -> 4% of each run, Pallas kernels for 0% -> 0%
where the time goes in v1:
time: 524 us
  waiting for transfers between devices  445 us (85%)
  blocking collectives  36 us (7%)
  matrix products  21.7 us (4%)
  between operations  14.2 us (3%)
  local copies, waits for them, and re-layouts  5.99 us (1%)
    reduce_scatter x1, waiting for transfers between devices, shards(): lax.psum_scatter((contract_cols(gate_grad, w_gate) + contract_cols(up_gra...  98.4 us
    unnamed x7, waiting for transfers between devices  76.4 us
    all_gather x1, waiting for transfers between devices, shards(): lax.all_gather(share_gate, 'row', axis=0, tiled=True)  73.7 us
    all_gather x1, waiting for transfers between devices, shards(): lax.all_gather(share_hidden, 'row', axis=0, tiled=True)  73.5 us
    all_gather x1, waiting for transfers between devices, shards(): lax.all_gather(share_up, 'row', axis=0, tiled=True)  71.2 us
    all_gather x1, waiting for transfers between devices, shards(): lax.all_gather(inputs, 'col', axis=0, tiled=True)  51.9 us
    all_to_all x1, blocking collectives, _clear_skins(): lax.all_to_all(jnp.stack([point] * lax.psum(1, 'col')), 'col', 0, 0)  36 us
    dot_general x3, matrix products, contract_cols(): lax.dot_general(left, right, (((1,), (1,)), ((), ())), preferred_element_...  11.4 us
  transfers between devices with their start and end apart: 6, of which 6 were waited for; matrix products, arithmetic and copies ran while one was open for 4% of the time, Pallas kernels for 0%

profile of v1, /device:TPU:2, one launch (start us, length us, event | category | flops | bytes accessed | tf_op | source)
XLA Modules:
  0.0 524.0 jit_solution(12223590343705402473)
XLA Ops:
  7.2 0.0 copy-start
  7.2 0.0 reduce-scatter.7.cloned.1.call-start
  7.2 1.1 stack.2
  8.3 0.0 copy-start.7
  8.4 36.0 %all_to_all.5 = bf16[32,64,512]{2,1,0:T(8,128)(2,1)S(1)} all-to-all(bf16[32,64,512]{2,1,0:T(8,128)(2,1)S(1)} %stack.2), channel_id=1, replica_groups=mesh['row'=16,'col'=32] {'col'}, dimensions={0} | all-to-all | bytes 4194304 | tf_op jit(solution)/shard_map/all_to_all | solution.py:36
  44.4 0.0 copy-start.2
  44.4 1.3 copy-done.2
  45.7 0.0 copy-done.7
  45.7 1.2 convolution_convert_fusion
  46.9 2.5 copy.11
  49.4 0.0 copy-start.4
  49.4 0.0 copy-start.5
  49.4 0.0 reduce-scatter.7.cloned.1.call-update
  49.4 0.0 all-gather.5.cloned.1.call-start
  49.5 74.7 %reduce-scatter.7.cloned.1.call-done = bf16[128,462]{1,0:T(8,128)(2,1)} async-done(((bf16[2048,462]{1,0:T(8,128)(2,1)}), bf16[128,462]{1,0:T(8,128)(2,1)}) %reduce-scatter.7.cloned.1.call-update) | async-done | bytes 118288
  124.1 1.0 copy.12
  125.2 0.0 copy-done.4
  125.2 0.0 copy-done.5
  125.2 0.9 fusion.6
  126.0 0.0 all-gather.5.cloned.1.call-update
  126.1 0.0 all-gather.7.cloned.1.call-start
  126.1 0.7 all-gather.7.cloned.1.call-update
  126.8 0.0 all-gather.9.cloned.1.call-start
  126.8 0.5 all-gather.9.cloned.1.call-update
  127.4 0.0 all-gather.11.cloned.1.call-start
  127.4 0.5 all-gather.11.cloned.1.call-update
  128.0 0.0 copy-start.3
  128.0 0.0 reduce-scatter.5.cloned.1.call-start
  128.0 73.7 %all-gather.5.cloned.1.call-done = bf16[2048,462]{0,1:T(8,128)(2,1)} async-done(((bf16[128,462]{0,1:T(8,128)(2,1)}), bf16[2048,462]{0,1:T(8,128)(2,1)}) %all-gather.5.cloned.1.call-update) | async-done | bytes 1892368 | tf_op jit(solution)/shard_map/all_gather | solution.py:53
  201.7 0.0 copy-done
  201.7 4.8 fusion.11
  206.5 71.2 %all-gather.7.cloned.1.call-done = bf16[2048,462]{0,1:T(8,128)(2,1)} async-done(((bf16[128,462]{0,1:T(8,128)(2,1)}), bf16[2048,462]{0,1:T(8,128)(2,1)}) %all-gather.7.cloned.1.call-update) | async-done | bytes 1892368 | tf_op jit(solution)/shard_map/all_gather | solution.py:54
  277.6 0.0 copy-done.3
  277.6 5.5 %add_convert_fusion = bf16[2048,512]{1,0:T(8,128)(2,1)} fusion(f32[2048,512]{1,0:T(8,128)} %fusion.11, bf16[2048,462]{0,1:T(8,128)(2,1)} %all-gather.7.cloned.1.call-done, bf16[512,462]{0,1:T(8,128)(2,1)S(1)} %copy-done.3), kind=kOutput, calls=%fused_computation | convolution fusion | flops 970981376 | bytes 8656896 | tf_op jit(solution)/shard_map/dot_general | solution.py:14
  283.1 0.0 reduce-scatter.5.cloned.1.call-update
  283.1 0.0 copy-start.1
  283.1 51.9 %all-gather.9.cloned.1.call-done = bf16[2048,512]{1,0:T(8,128)(2,1)} async-done(((bf16[64,512]{1,0:T(8,128)(2,1)}), bf16[2048,512]{1,0:T(8,128)(2,1)}) %all-gather.9.cloned.1.call-update) | async-done | bytes 2097168 | tf_op jit(solution)/shard_map/all_gather | solution.py:42
  335.1 0.0 copy-start.6
  335.1 4.2 fusion.1
  339.3 0.0 copy-done.1
  339.3 0.0 copy-done.6
  339.3 1.9 fusion
  341.2 73.5 %all-gather.11.cloned.1.call-done = bf16[2048,462]{0,1:T(8,128)(2,1)} async-done(((bf16[128,462]{0,1:T(8,128)(2,1)}), bf16[2048,462]{0,1:T(8,128)(2,1)}) %all-gather.11.cloned.1.call-update) | async-done | bytes 1892368 | tf_op jit(solution)/shard_map/all_gather | solution.py:52
  414.7 4.1 convolution_convert_fusion.1
  418.8 98.4 %reduce-scatter.5.cloned.1.call-done = bf16[64,512]{1,0:T(8,128)(2,1)} async-done(((bf16[2048,512]{1,0:T(8,128)(2,1)}), bf16[64,512]{1,0:T(8,128)(2,1)}) %reduce-scatter.5.cloned.1.call-update) | async-done | bytes 65552 | tf_op jit(solution)/shard_map/reduce_scatter | solution.py:59
Async XLA Ops:
  7.2 194.6 %copy-start = (bf16[512,462]{0,1:T(8,128)(2,1)S(1)}, bf16[512,462]{0,1:T(8,128)(2,1)}, u32[]{:S(2)}) copy-start(bf16[512,462]{0,1:T(8,128)(2,1)} %param.10) | copy-start | bytes 1419268
  7.2 116.9 %reduce-scatter.7.cloned.1.call-start = ((), (), s32[]{:S(2)}) async-start(), calls=%async_computation.8 | async-start | bytes 2228224
  8.3 37.4 %copy-start.7 = (bf16[462,512]{1,0:T(8,128)(2,1)S(1)}, bf16[462,512]{1,0:T(8,128)(2,1)}, u32[]{:S(2)}) copy-start(bf16[462,512]{1,0:T(8,128)(2,1)} %param.12) | copy-start | bytes 1419268
  44.4 1.3 copy-start.2
  49.4 75.8 %copy-start.4 = (bf16[128,462]{0,1:T(8,128)(2,1)S(1)}, bf16[128,462]{0,1:T(8,128)(2,1)}, u32[]{:S(2)}) copy-start(bf16[128,462]{0,1:T(8,128)(2,1)} %param.9) | copy-start | bytes 354820
  49.4 75.8 %copy-start.5 = (bf16[128,462]{0,1:T(8,128)(2,1)S(1)}, bf16[128,462]{0,1:T(8,128)(2,1)}, u32[]{:S(2)}) copy-start(bf16[128,462]{0,1:T(8,128)(2,1)} %param.8) | copy-start | bytes 354820
  49.4 152.3 %all-gather.5.cloned.1.call-start = ((), (), s32[]{:S(2)}) async-start(), calls=%async_computation.3 | async-start | bytes 2019328 | tf_op jit(solution)/shard_map/all_gather | solution.py:53
  126.1 151.6 %all-gather.7.cloned.1.call-start = ((), (), s32[]{:S(2)}) async-start(), calls=%async_computation.4 | async-start | bytes 2019328 | tf_op jit(solution)/shard_map/all_gather | solution.py:54
  126.8 208.3 %all-gather.9.cloned.1.call-start = ((), (), s32[]{:S(2)}) async-start(), calls=%async_computation.6 | async-start | bytes 2162688 | tf_op jit(solution)/shard_map/all_gather | solution.py:42
  127.4 287.4 %all-gather.11.cloned.1.call-start = ((), (), s32[]{:S(2)}) async-start(), calls=%async_computation.7 | async-start | bytes 2019328 | tf_op jit(solution)/shard_map/all_gather | solution.py:52
  128.0 149.7 %copy-start.3 = (bf16[512,462]{0,1:T(8,128)(2,1)S(1)}, bf16[512,462]{0,1:T(8,128)(2,1)}, u32[]{:S(2)}) copy-start(bf16[512,462]{0,1:T(8,128)(2,1)} %param.11) | copy-start | bytes 1419268
  128.0 389.2 %reduce-scatter.5.cloned.1.call-start = ((), (), s32[]{:S(2)}) async-start(), calls=%async_computation.5 | async-start | bytes 2162688 | tf_op jit(solution)/shard_map/reduce_scatter | solution.py:59
  283.1 56.2 %copy-start.1 = (bf16[2048,462]{0,1:T(8,128)(2,1)S(1)}, bf16[2048,462]{0,1:T(8,128)(2,1)}, u32[]{:S(2)}) copy-start(bf16[2048,462]{0,1:T(8,128)(2,1)} %all-gather.5.cloned.1.call-done) | copy-start | bytes 5677060
  335.1 4.2 copy-start.6
Sparse Core Ops, SparseCore 0:
  49.5 74.5 reduce-scatter.6
  126.7 74.9 all-gather.4
  204.3 73.2 all-gather.6
  280.6 54.3 all-gather.8
  337.5 77.2 all-gather.10
  419.6 97.5 reduce-scatter.4
